TPU v7x, 256 devices: a whole 4x4x8 slice. The times are simulated.
256 devices in a mesh: section: 16 (over x, z_lo, core), dp: 16 (over z_hi, y).
Axes of the slice: x: 4, y: 4, z: 8 (z_hi: 4, z_lo: 2; z = z_hi * 2 + z_lo), core: 2. Of those that a mesh axis runs over, the one named last changes fastest.
Arguments:
- encoder_out: bfloat16 [2, 2, 256, 4096], P(None, None, 'dp', 'section'), may hold values from -6 to 6
- encoder_len: int32 [2, 2], replicated, may hold values from 1 to 2, as said below
- decoder_len: int32 [2, 2], replicated, may hold values from 1 to 2, as said below
- queries: bfloat16 [16, 2, 2, 256, 4096], P('section', None, None, None, 'dp'), may hold values from -40 to 40
- cotangent: bfloat16 [16, 2, 2, 256, 4096], P('section', None, None, None, 'dp'), may hold values from -6 to 6
- key_weight: bfloat16 [16, 4096, 4096], P('section', None, 'dp'), may hold values from -0.09375 to 0.09375
- value_weight: bfloat16 [16, 4096, 4096], P('section', None, 'dp'), may hold values from -0.09375 to 0.09375
Outputs:
- attention: bfloat16 [16, 2, 2, 256, 4096], P('section', None, None, None, 'dp')
- grad_query: bfloat16 [16, 2, 2, 256, 4096], P('section', None, None, None, 'dp')
- grad_key_weight: bfloat16 [16, 4096, 4096], P('section', None, 'dp')
- grad_value_weight: bfloat16 [16, 4096, 4096], P('section', None, 'dp')
- grad_encoder: float32 [2, 2, 256, 4096], P(None, None, 'dp', 'section')
Inputs may be any that keep to these rules, and one draw needn't show every extreme that they name: `encoder_len`: in every micro-batch some example fills all 2 encoder blocks. `decoder_len`: in every micro-batch some example fills all 2 decoder blocks.
All inputs are finite; a program needn't handle non-finite values.
Results may differ from a plain program's by a relative error of at most 0.012.
The roundings to bfloat16 on the way count: a program that leaves them out, or rounds other values in their place, can miss the bound.
Values may be sent and summed in bfloat16 or wider, within the bound.
No kernel may reach another device: no remote copies, remote signals or barrier semaphores. Data moves between devices by JAX's collectives and lax.ppermute only.
A program may use at most 128 MiB of HBM per device.

v0:
```python
import jax
import jax.numpy as jnp
from jax import lax
from jax.sharding import PartitionSpec as P

HD = 256
BLOCK = 128
ENC_BLOCKS = 2
MICRO = 2
NEG_FILL = -1e30


def attend(query_rows, key_rows, value_rows, cotan_rows, key_valid, query_valid):
    score_scale = HD ** (-0.5)
    scores = (
        jnp.einsum("eqhd,ekhd->ehqk", query_rows, key_rows, preferred_element_type=jnp.float32)
        * score_scale
    )
    scores = jnp.where(key_valid[:, None, None, :], scores, NEG_FILL)
    largest = jnp.max(scores, axis=-1, keepdims=True)
    weights = jnp.exp(scores - largest)
    probs = weights / jnp.sum(weights, axis=-1, keepdims=True)
    probs_low = probs.astype(jnp.bfloat16)
    attended = jnp.einsum(
        "ehqk,ekhd->eqhd", probs_low, value_rows, preferred_element_type=jnp.float32
    )
    attended = jnp.where(query_valid[:, :, None, None], attended, 0.0).astype(jnp.bfloat16)
    cotan_kept = jnp.where(query_valid[:, :, None, None], cotan_rows, jnp.zeros_like(cotan_rows))
    grad_value = jnp.einsum(
        "ehqk,eqhd->ekhd", probs_low, cotan_kept, preferred_element_type=jnp.float32
    ).astype(jnp.bfloat16)
    grad_probs = jnp.einsum(
        "eqhd,ekhd->ehqk", cotan_kept, value_rows, preferred_element_type=jnp.float32
    )
    inner_sum = jnp.sum(probs * grad_probs, axis=-1, keepdims=True)
    grad_scores = (probs * (grad_probs - inner_sum) * score_scale).astype(jnp.bfloat16)
    grad_query = jnp.einsum(
        "ehqk,ekhd->eqhd", grad_scores, key_rows, preferred_element_type=jnp.float32
    ).astype(jnp.bfloat16)
    grad_key = jnp.einsum(
        "ehqk,eqhd->ekhd", grad_scores, query_rows, preferred_element_type=jnp.float32
    ).astype(jnp.bfloat16)
    return (attended, grad_query, grad_key, grad_value)


def body(encoder_out, encoder_len, decoder_len, queries, cotangent, key_weight, value_weight):
    key_mat = key_weight[0]
    value_mat = value_weight[0]
    width_dev = key_mat.shape[1]
    heads_dev = width_dev // HD
    enc_rows = ENC_BLOCKS * BLOCK
    dec_rows = queries.shape[3]
    examples = queries.shape[2]
    rows_dev = enc_rows // lax.axis_size("dp")
    key_positions = jnp.arange(enc_rows, dtype=jnp.int32)
    query_positions = jnp.arange(dec_rows, dtype=jnp.int32)
    key_acc = jnp.zeros(key_mat.shape, jnp.float32)
    value_acc = jnp.zeros(value_mat.shape, jnp.float32)
    attn_list, query_list, encoder_list = ([], [], [])
    groups = lax.axis_size("dp")
    copies = jnp.broadcast_to(encoder_out[None], (groups,) + encoder_out.shape)
    from_each = lax.all_to_all(copies, "dp", 0, 0, tiled=True)
    tall_enc = jnp.moveaxis(from_each, 0, 2).reshape(
        encoder_out.shape[:2] + (groups * encoder_out.shape[2], encoder_out.shape[3])
    )
    gathered_enc = lax.all_gather(tall_enc, "section", axis=3, tiled=True)
    for micro_idx in range(MICRO):
        whole_enc = gathered_enc[micro_idx]
        key_rows = jnp.einsum(
            "ekd,dc->ekc", whole_enc, key_mat, preferred_element_type=jnp.float32
        ).astype(jnp.bfloat16)
        value_rows = jnp.einsum(
            "ekd,dc->ekc", whole_enc, value_mat, preferred_element_type=jnp.float32
        ).astype(jnp.bfloat16)
        key_valid = key_positions[None, :] < (BLOCK * encoder_len[micro_idx])[:, None]
        query_valid = query_positions[None, :] < (BLOCK * decoder_len[micro_idx])[:, None]
        attended, grad_query, grad_key, grad_value = attend(
            queries[0, micro_idx].reshape(examples, dec_rows, heads_dev, HD),
            key_rows.reshape(examples, enc_rows, heads_dev, HD),
            value_rows.reshape(examples, enc_rows, heads_dev, HD),
            cotangent[0, micro_idx].reshape(examples, dec_rows, heads_dev, HD),
            key_valid,
            query_valid,
        )
        key_flat = grad_key.reshape(examples, enc_rows, width_dev)
        value_flat = grad_value.reshape(examples, enc_rows, width_dev)
        key_acc = key_acc + jnp.einsum(
            "ekd,ekc->dc", whole_enc, key_flat, preferred_element_type=jnp.float32
        )
        value_acc = value_acc + jnp.einsum(
            "ekd,ekc->dc", whole_enc, value_flat, preferred_element_type=jnp.float32
        )
        sections = lax.axis_size("section")
        key_blocks = key_mat.reshape(sections, key_mat.shape[0] // sections, width_dev)
        value_blocks = value_mat.reshape(sections, value_mat.shape[0] // sections, width_dev)
        feature_blocks = (
            jnp.einsum("ekc,fdc->fked", key_flat, key_blocks, preferred_element_type=jnp.float32)
            + jnp.einsum(
                "ekc,fdc->fked", value_flat, value_blocks, preferred_element_type=jnp.float32
            )
        ).astype(jnp.bfloat16)
        from_sections = lax.all_to_all(feature_blocks, "section", 0, 0, tiled=True)
        encoder_list.append(jnp.sum(from_sections.astype(jnp.float32), axis=0))
        attn_list.append(attended.reshape(examples, dec_rows, width_dev))
        query_list.append(grad_query.reshape(examples, dec_rows, width_dev))
    attention = jnp.stack(attn_list)[None]
    query_grads = jnp.stack(query_list)[None]
    key_grads = key_acc.astype(jnp.bfloat16)[None]
    value_grads = value_acc.astype(jnp.bfloat16)[None]
    section_share = jnp.stack(encoder_list)
    micro, enc_rows_all, examples_all, width_sec = section_share.shape
    row_blocks = section_share.reshape(
        micro, groups, enc_rows_all // groups, examples_all, width_sec
    ).transpose(1, 0, 3, 2, 4)
    received = lax.all_to_all(row_blocks, "dp", 0, 0, tiled=True)
    grad_encoder = jnp.sum(received, axis=0)
    return (attention, query_grads, key_grads, value_grads, grad_encoder)


def solution(mesh):
    placed = (
        P(None, None, "dp", "section"),
        P(),
        P(),
        P("section", None, None, None, "dp"),
        P("section", None, None, None, "dp"),
        P("section", None, "dp"),
        P("section", None, "dp"),
    )
    return jax.shard_map(
        body,
        mesh=mesh,
        in_specs=placed,
        out_specs=(
            P("section", None, None, None, "dp"),
            P("section", None, None, None, "dp"),
            P("section", None, "dp"),
            P("section", None, "dp"),
            P(None, None, "dp", "section"),
        ),
        check_vma=False,
    )
```

profile of v0, /device:TPU:32, one launch (start us, length us, event | category | flops | bytes accessed | tf_op | source)
XLA Modules:
  0.0 275.1 jit_solution(1751855742102394611)
XLA Ops:
  8.2 27.6 %all_to_all.20 = bf16[16,2,2,16,256]{4,3,2,1,0:T(8,128)(2,1)S(1)} all-to-all(bf16[16,2,2,16,256]{4,3,2,1,0:T(8,128)(2,1)S(1)} %broadcast_in_dim.88), channel_id=1, replica_groups=mesh['section'=16,'dp'=16] {'dp'}, dimensions={0} | all-to-all | bytes 1048576 | tf_op jit(solution)/shard_map/all_to_all | solution.py:62
  38.3 59.1 %all-gather.2.cloned.1.call-done = bf16[2,2,256,4096]{3,2,1,0:T(8,128)(2,1)} async-done(((bf16[2,2,256,256]{3,2,1,0:T(8,128)(2,1)}), bf16[2,2,256,4096]{3,2,1,0:T(8,128)(2,1)}) %all-gather.2.cloned.1.call-update) | async-done | bytes 8388624 | tf_op jit(solution)/shard_map/all_gather | solution.py:66
  97.4 4.2 %fusion.42 = bf16[2,256,256]{2,1,0:T(8,128)(2,1)S(1)} fusion(bf16[1,4096,256]{2,1,0:T(8,128)(2,1)} %param.13, bf16[2,2,256,4096]{3,2,1,0:T(8,128)(2,1)} %all-gather.2.cloned.1.call-done), kind=kOutput, calls=%fused_computation.52 | convolution fusion | flops 1073872896 | bytes 6553600 | tf_op jit(solution)/shard_map/ekd,dc->ekc/dot_general | solution.py:72
  112.0 2.2 copy.81
  114.2 4.9 %all-to-all-start.1 = ((bf16[16,256,2,256]{3,1,2,0:T(8,128)(2,1)}), bf16[16,256,2,256]{3,1,2,0:T(8,128)(2,1)}, u32[]{:S(2)}, u32[]{:S(2)}) async-start(bf16[16,256,2,256]{3,1,2,0:T(8,128)(2,1)} %copy.81), calls=%async_computation.1 | async-start | bytes 8388608 | tf_op jit(solution)/shard_map/all_to_all | solution.py:102
  119.1 4.1 %fusion.36 = bf16[2,256,256]{2,1,0:T(8,128)(2,1)S(1)} fusion(bf16[1,4096,256]{2,1,0:T(8,128)(2,1)} %param.13, bf16[2,2,256,4096]{3,2,1,0:T(8,128)(2,1)} %all-gather.2.cloned.1.call-done), kind=kOutput, calls=%fused_computation.50 | convolution fusion | flops 1073872896 | bytes 6553600 | tf_op jit(solution)/shard_map/ekd,dc->ekc/dot_general | solution.py:72
  124.4 3.4 %fusion.39 = bf16[2,256,256]{2,1,0:T(8,128)(2,1)S(1)} fusion(bf16[1,4096,256]{2,1,0:T(8,128)(2,1)S(1)} %copy-done, bf16[2,2,256,4096]{3,2,1,0:T(8,128)(2,1)} %all-gather.2.cloned.1.call-done), kind=kOutput, calls=%fused_computation.51 | convolution fusion | flops 1073872896 | bytes 6553600 | tf_op jit(solution)/shard_map/ekd,dc->ekc/dot_general | solution.py:69
  127.8 2.2 fusion.126
  136.7 2.2 copy.84
  139.0 29.4 %all-to-all-done.1 = bf16[16,256,2,256]{3,1,2,0:T(8,128)(2,1)} async-done(((bf16[16,256,2,256]{3,1,2,0:T(8,128)(2,1)}), bf16[16,256,2,256]{3,1,2,0:T(8,128)(2,1)}, u32[]{:S(2)}, u32[]{:S(2)}) %all-to-all-start.1) | async-done | bytes 4194336 | tf_op jit(solution)/shard_map/all_to_all | solution.py:102
  168.3 5.6 %all-to-all-start.2 = ((bf16[16,256,2,256]{3,1,2,0:T(8,128)(2,1)}), bf16[16,256,2,256]{3,1,2,0:T(8,128)(2,1)}, u32[]{:S(2)}, u32[]{:S(2)}) async-start(bf16[16,256,2,256]{3,1,2,0:T(8,128)(2,1)} %copy.84), calls=%async_computation.2 | async-start | bytes 8388608 | tf_op jit(solution)/shard_map/all_to_all | solution.py:102
  176.3 2.1 fusion.52
  178.3 2.6 fusion.53
  181.0 2.8 %convert_reduce_fusion.1 = f32[256,2,256]{2,0,1:T(8,128)S(1)} fusion(bf16[16,256,2,256]{3,1,2,0:T(8,128)(2,1)} %all-to-all-done.1), kind=kLoop, calls=%fused_computation.6 | loop fusion | flops 4063232 | bytes 4718592 | tf_op jit(solution)/shard_map/reduce_sum | solution.py:103
  184.2 39.0 %all-to-all-done.2 = bf16[16,256,2,256]{3,1,2,0:T(8,128)(2,1)} async-done(((bf16[16,256,2,256]{3,1,2,0:T(8,128)(2,1)}), bf16[16,256,2,256]{3,1,2,0:T(8,128)(2,1)}, u32[]{:S(2)}, u32[]{:S(2)}) %all-to-all-start.2) | async-done | bytes 4194336 | tf_op jit(solution)/shard_map/all_to_all | solution.py:102
  223.2 2.8 %convert_reduce_fusion = f32[256,2,256]{2,0,1:T(8,128)S(1)} fusion(bf16[16,256,2,256]{3,1,2,0:T(8,128)(2,1)} %all-to-all-done.2), kind=kLoop, calls=%fused_computation.4 | loop fusion | flops 4063232 | bytes 4718592 | tf_op jit(solution)/shard_map/reduce_sum | solution.py:103
  228.3 8.2 %all-to-all-start.3 = ((f32[16,2,2,16,256]{4,2,3,1,0:T(2,128)}), f32[16,2,2,16,256]{4,2,3,1,0:T(2,128)S(1)}, u32[]{:S(2)}, u32[]{:S(2)}) async-start(f32[16,2,2,16,256]{4,2,3,1,0:T(2,128)} %maximum_bitcast_fusion), calls=%async_computation.3 | async-start | bytes 2097152 | tf_op jit(solution)/shard_map/all_to_all | solution.py:115
  238.5 3.6 %convolution_bitcast_fusion.2 = f32[256,4096]{1,0:T(8,128)S(1)} fusion(bf16[2,256,256]{2,1,0:T(8,128)(2,1)S(1)} %copy-done.8, bf16[2,2,256,4096]{3,2,1,0:T(8,128)(2,1)} %all-gather.2.cloned.1.call-done), kind=kOutput, calls=%fused_computation.10 | convolution fusion | flops 1073741824 | bytes 8650752 | tf_op jit(solution)/shard_map/ekd,ekc->dc/dot_general | solution.py:87
  242.0 3.6 %fusion.8 = bf16[1,4096,256]{1,2,0:T(8,128)(2,1)S(1)} fusion(f32[256,4096]{1,0:T(8,128)S(1)} %convolution_bitcast_fusion.2, bf16[2,256,256]{2,1,0:T(8,128)(2,1)S(1)} %copy-done.10, bf16[2,2,256,4096]{3,2,1,0:T(8,128)(2,1)} %all-gather.2.cloned.1.call-done), kind=kOutput, calls=%fused_computation.16 | convolution fusion | flops 1075838976 | bytes 10747904 | tf_op jit(solution)/shard_map/ekd,ekc->dc/dot_general | solution.py:87
  245.7 2.5 copy.90
  248.1 3.5 %convolution_bitcast_fusion = f32[256,4096]{1,0:T(8,128)S(1)} fusion(bf16[2,2,256,4096]{3,2,1,0:T(8,128)(2,1)} %all-gather.2.cloned.1.call-done, bf16[2,256,256]{2,1,0:T(8,128)(2,1)S(1)} %convolution_convert_fusion), kind=kOutput, calls=%fused_computation.8 | convolution fusion | flops 1073741824 | bytes 8650752 | tf_op jit(solution)/shard_map/ekd,ekc->dc/dot_general | solution.py:90
  251.6 5.1 %fusion.9 = bf16[1,4096,256]{1,2,0:T(8,128)(2,1)} fusion(f32[256,4096]{1,0:T(8,128)S(1)} %convolution_bitcast_fusion, bf16[2,2,256,4096]{3,2,1,0:T(8,128)(2,1)} %all-gather.2.cloned.1.call-done, bf16[2,256,256]{2,1,0:T(8,128)(2,1)S(1)} %copy-done.6), kind=kOutput, calls=%fused_computation.17 | convolution fusion | flops 1075838976 | bytes 10747904 | tf_op jit(solution)/shard_map/ekd,ekc->dc/dot_general | solution.py:90
  256.7 4.1 %copy.91 = bf16[1,4096,256]{2,1,0:T(8,128)(2,1)} copy(bf16[1,4096,256]{1,2,0:T(8,128)(2,1)} %fusion.9) | data formatting | bytes 4194304
  260.8 6.4 %all-to-all-done.3 = f32[16,2,2,16,256]{4,2,3,1,0:T(2,128)S(1)} async-done(((f32[16,2,2,16,256]{4,2,3,1,0:T(2,128)}), f32[16,2,2,16,256]{4,2,3,1,0:T(2,128)S(1)}, u32[]{:S(2)}, u32[]{:S(2)}) %all-to-all-start.3) | async-done | bytes 1048608 | tf_op jit(solution)/shard_map/all_to_all | solution.py:115
  (71 shorter events, 29.5 us)
Async XLA Ops:
  7.2 95.6 %copy-start = (bf16[1,4096,256]{2,1,0:T(8,128)(2,1)S(1)}, bf16[1,4096,256]{2,1,0:T(8,128)(2,1)}, u32[]{:S(2)}) copy-start(bf16[1,4096,256]{2,1,0:T(8,128)(2,1)} %param.12) | copy-start | bytes 6291460
  7.2 90.2 %all-gather.2.cloned.1.call-start = ((), (), s32[]{:S(2)}) async-start(), calls=%async_computation.4 | async-start | bytes 8912896 | tf_op jit(solution)/shard_map/all_gather | solution.py:66
  38.3 63.4 %copy-start.11 = (bf16[1,2,2,256,256]{4,3,2,1,0:T(8,128)(2,1)S(1)}, bf16[1,2,2,256,256]{4,3,2,1,0:T(8,128)(2,1)}, u32[]{:S(2)}) copy-start(bf16[1,2,2,256,256]{4,3,2,1,0:T(8,128)(2,1)} %param.11) | copy-start | bytes 1572868
  97.4 5.4 %copy-start.2 = (bf16[2,2,256,4096]{3,2,1,0:T(8,128)(2,1)S(1)}, bf16[2,2,256,4096]{3,2,1,0:T(8,128)(2,1)}, u32[]{:S(2)}) copy-start(bf16[2,2,256,4096]{3,2,1,0:T(8,128)(2,1)} %all-gather.2.cloned.1.call-done) | copy-start | bytes 25165828
  101.6 2.5 copy-start.12
  102.8 1.3 copy-start.14
  104.1 6.2 %copy-start.16 = (bf16[2,256,256]{2,1,0:T(8,128)(2,1)}, bf16[2,256,256]{2,1,0:T(8,128)(2,1)S(1)}, u32[]{:S(2)}) copy-start(bf16[2,256,256]{2,1,0:T(8,128)(2,1)S(1)} %fusion.45) | copy-start | bytes 786436
  106.9 3.4 %copy-start.5 = (bf16[2,256,256]{2,1,0:T(8,128)(2,1)}, bf16[2,256,256]{2,1,0:T(8,128)(2,1)S(1)}, u32[]{:S(2)}) copy-start(bf16[2,256,256]{2,1,0:T(8,128)(2,1)S(1)} %convolution_convert_fusion.1) | copy-start | bytes 786436
  108.9 1.3 copy-start.9
  109.0 1.7 copy-start.3
  114.2 54.2 %all-to-all-start.1 = ((bf16[16,256,2,256]{3,1,2,0:T(8,128)(2,1)}), bf16[16,256,2,256]{3,1,2,0:T(8,128)(2,1)}, u32[]{:S(2)}, u32[]{:S(2)}) async-start(bf16[16,256,2,256]{3,1,2,0:T(8,128)(2,1)} %copy.81), calls=%async_computation.1 | async-start | bytes 8388608 | tf_op jit(solution)/shard_map/all_to_all | solution.py:102
  127.8 2.2 copy-start.18
  132.0 3.1 %copy-start.7 = (bf16[2,256,256]{2,1,0:T(8,128)(2,1)}, bf16[2,256,256]{2,1,0:T(8,128)(2,1)S(1)}, u32[]{:S(2)}) copy-start(bf16[2,256,256]{2,1,0:T(8,128)(2,1)S(1)} %convolution_convert_fusion.2) | copy-start | bytes 786436
  133.8 1.6 copy-start.4
  138.9 35.0 %copy-start.13 = (bf16[2,256,256]{2,1,0:T(8,128)(2,1)S(1)}, bf16[2,256,256]{2,1,0:T(8,128)(2,1)}, u32[]{:S(2)}) copy-start(bf16[2,256,256]{2,1,0:T(8,128)(2,1)} %copy-done.12) | copy-start | bytes 786436
  139.0 35.0 %copy-start.15 = (bf16[1,2,2,256,256]{4,3,2,1,0:T(8,128)(2,1)S(1)}, bf16[1,2,2,256,256]{4,3,2,1,0:T(8,128)(2,1)}, u32[]{:S(2)}) copy-start(bf16[1,2,2,256,256]{4,3,2,1,0:T(8,128)(2,1)} %param.10) | copy-start | bytes 1572868
  139.0 35.0 %copy-start.17 = (bf16[2,256,256]{2,1,0:T(8,128)(2,1)S(1)}, bf16[2,256,256]{2,1,0:T(8,128)(2,1)}, u32[]{:S(2)}) copy-start(bf16[2,256,256]{2,1,0:T(8,128)(2,1)} %copy-done.16) | copy-start | bytes 786436
  139.0 35.6 %copy-start.19 = (bf16[2,256,256]{2,1,0:T(8,128)(2,1)S(1)}, bf16[2,256,256]{2,1,0:T(8,128)(2,1)}, u32[]{:S(2)}) copy-start(bf16[2,256,256]{2,1,0:T(8,128)(2,1)} %copy-done.18) | copy-start | bytes 786436
  168.3 54.8 %all-to-all-start.2 = ((bf16[16,256,2,256]{3,1,2,0:T(8,128)(2,1)}), bf16[16,256,2,256]{3,1,2,0:T(8,128)(2,1)}, u32[]{:S(2)}, u32[]{:S(2)}) async-start(bf16[16,256,2,256]{3,1,2,0:T(8,128)(2,1)} %copy.84), calls=%async_computation.2 | async-start | bytes 8388608 | tf_op jit(solution)/shard_map/all_to_all | solution.py:102
  226.0 12.4 %copy-start.8 = (bf16[2,256,256]{2,1,0:T(8,128)(2,1)S(1)}, bf16[2,256,256]{2,1,0:T(8,128)(2,1)}, u32[]{:S(2)}) copy-start(bf16[2,256,256]{2,1,0:T(8,128)(2,1)} %copy-done.7) | copy-start | bytes 786436
  228.3 38.9 %all-to-all-start.3 = ((f32[16,2,2,16,256]{4,2,3,1,0:T(2,128)}), f32[16,2,2,16,256]{4,2,3,1,0:T(2,128)S(1)}, u32[]{:S(2)}, u32[]{:S(2)}) async-start(f32[16,2,2,16,256]{4,2,3,1,0:T(2,128)} %maximum_bitcast_fusion), calls=%async_computation.3 | async-start | bytes 2097152 | tf_op jit(solution)/shard_map/all_to_all | solution.py:115
  238.5 3.6 %copy-start.10 = (bf16[2,256,256]{2,1,0:T(8,128)(2,1)S(1)}, bf16[2,256,256]{2,1,0:T(8,128)(2,1)}, u32[]{:S(2)}) copy-start(bf16[2,256,256]{2,1,0:T(8,128)(2,1)} %copy-done.9) | copy-start | bytes 786436
  248.1 3.5 %copy-start.6 = (bf16[2,256,256]{2,1,0:T(8,128)(2,1)S(1)}, bf16[2,256,256]{2,1,0:T(8,128)(2,1)}, u32[]{:S(2)}) copy-start(bf16[2,256,256]{2,1,0:T(8,128)(2,1)} %copy-done.5) | copy-start | bytes 786436
  251.6 16.6 %copy-start.1 = (bf16[1,4096,256]{2,1,0:T(8,128)(2,1)S(1)}, bf16[1,4096,256]{2,1,0:T(8,128)(2,1)}, u32[]{:S(2)}) copy-start(bf16[1,4096,256]{2,1,0:T(8,128)(2,1)} %param.12) | copy-start | bytes 6291460
Sparse Core Ops, SparseCore 0:
  36.7 60.6 all-gather.1
where the time goes:
time: 276 us; the launch traced here: 275 us
  waiting for transfers between devices  134 us (49%)
  matrix products  52.9 us (19%)
  blocking collectives  27.6 us (10%)
  starting transfers between devices  18.8 us (7%)
  local copies, waits for them, and re-layouts  16.9 us (6%)
  between operations  14.4 us (5%)
  other arithmetic  10.6 us (4%)
    all_to_all x2, waiting for transfers between devices, body(): from_sections = lax.all_to_all(feature_blocks, 'section', 0, 0, tiled=True)  68.4 us
    all_gather x1, waiting for transfers between devices, body(): gathered_enc = lax.all_gather(tall_enc, 'section', axis=3, tiled=True)  59.1 us
    all_to_all x1, blocking collectives, body(): from_each = lax.all_to_all(copies, 'dp', 0, 0, tiled=True)  27.6 us
    all_to_all x2, starting transfers between devices, body(): from_sections = lax.all_to_all(feature_blocks, 'section', 0, 0, tiled=True)  10.6 us
    unnamed x45, local copies, waits for them, and re-layouts  9.88 us
    dot_general x2, matrix products, body(): jnp.einsum('ekd,ekc->dc', whole_enc, value_flat, preferred_element_type=j...  8.57 us
    dot_general x2, matrix products, body(): jnp.einsum('ekd,dc->ekc', whole_enc, value_mat, preferred_element_type=jn...  8.36 us
    all_to_all x1, starting transfers between devices, body(): received = lax.all_to_all(row_blocks, 'dp', 0, 0, tiled=True)  8.18 us
  transfers between devices with their start and end apart: 4, of which 4 were waited for; matrix products, arithmetic and copies ran while one was open for 20% of the time, Pallas kernels for 0%

commit v1 on v0

--- a/solution.py
+++ b/solution.py
@@ -63,7 +63,9 @@
     tall_enc = jnp.moveaxis(from_each, 0, 2).reshape(
         encoder_out.shape[:2] + (groups * encoder_out.shape[2], encoder_out.shape[3])
     )
-    gathered_enc = lax.all_gather(tall_enc, "section", axis=3, tiled=True)
+    gathered_enc = jnp.concatenate(
+        lax.all_to_all(jnp.stack([tall_enc] * lax.axis_size("section")), "section", 0, 0), axis=3
+    )
     for micro_idx in range(MICRO):
         whole_enc = gathered_enc[micro_idx]
         key_rows = jnp.einsum(

time: 276 us -> 320 us (1.16)
  local copies, waits for them, and re-layouts: 16.9 us -> 56.2 us
  waiting for transfers between devices: 134 us -> 149 us
  between operations: 14.4 us -> 0.96 us
    all_to_all x0 -> x1, waiting for transfers between devices: none -> 93.9 us  [body(): lax.all_to_all(jnp.stack([tall_enc] * lax.axis_size('section')), 'section...]
    all_gather x1 -> x0, waiting for transfers between devices: 59.1 us -> none  [body(): gathered_enc = lax.all_gather(tall_enc, 'section', axis=3, tiled=True)]
    slice x0 -> x3, local copies, waits for them, and re-layouts: none -> 16.1 us  [body(): whole_enc = gathered_enc[micro_idx]]
    all_to_all x2, waiting for transfers between devices: 68.4 us -> 53.1 us  [body(): from_sections = lax.all_to_all(feature_blocks, 'section', 0, 0, tiled=True)]
    squeeze x0 -> x2, local copies, waits for them, and re-layouts: none -> 14.8 us  [body(): whole_enc = gathered_enc[micro_idx]]
    all_to_all x0 -> x1, starting transfers between devices: none -> 5.91 us  [body(): lax.all_to_all(jnp.stack([tall_enc] * lax.axis_size('section')), 'section...]
    unnamed x45 -> x49, local copies, waits for them, and re-layouts: 9.88 us -> 14.8 us
    another operation x0 -> x1, local copies, waits for them, and re-layouts: none -> 4.22 us  [body(): jnp.stack([tall_enc] * lax.axis_size('section'))]
  transfers between devices with their start and end apart: 4 -> 4, of which waited for: 4 -> 4; matrix products, arithmetic and copies ran while one was open for 20% -> 23% of each run, Pallas kernels for 0% -> 0%
where the time goes in v1:
time: 320 us; the launch traced here: 319 us
  waiting for transfers between devices  149 us (47%)
  local copies, waits for them, and re-layouts  56.2 us (18%)
  matrix products  51.6 us (16%)
  blocking collectives  27.6 us (9%)
  starting transfers between devices  21.8 us (7%)
  other arithmetic  11.6 us (4%)
    all_to_all x1, waiting for transfers between devices, body(): lax.all_to_all(jnp.stack([tall_enc] * lax.axis_size('section')), 'section...  93.9 us
    all_to_all x2, waiting for transfers between devices, body(): from_sections = lax.all_to_all(feature_blocks, 'section', 0, 0, tiled=True)  53.1 us
    all_to_all x1, blocking collectives, body(): from_each = lax.all_to_all(copies, 'dp', 0, 0, tiled=True)  27.6 us
    slice x3, local copies, waits for them, and re-layouts, body(): whole_enc = gathered_enc[micro_idx]  16.1 us
    unnamed x49, local copies, waits for them, and re-layouts  14.8 us
    squeeze x2, local copies, waits for them, and re-layouts, body(): whole_enc = gathered_enc[micro_idx]  14.8 us
    all_to_all x2, starting transfers between devices, body(): from_sections = lax.all_to_all(feature_blocks, 'section', 0, 0, tiled=True)  11.2 us
  transfers between devices with their start and end apart: 4, of which 4 were waited for; matrix products, arithmetic and copies ran while one was open for 23% of the time, Pallas kernels for 0%

profile of v1, /device:TPU:32, one launch (start us, length us, event | category | flops | bytes accessed | tf_op | source)
XLA Modules:
  0.0 318.9 jit_solution(12827776979003886267)
XLA Ops:
  1.6 27.6 %all_to_all.25 = bf16[16,2,2,16,256]{4,3,2,1,0:T(8,128)(2,1)S(1)} all-to-all(bf16[16,2,2,16,256]{4,3,2,1,0:T(8,128)(2,1)S(1)} %broadcast_in_dim.88), channel_id=1, replica_groups=mesh['section'=16,'dp'=16] {'dp'}, dimensions={0} | all-to-all | bytes 1048576 | tf_op jit(solution)/shard_map/all_to_all | solution.py:62
  29.2 4.2 %stack.18 = bf16[16,2,2,256,256]{4,3,2,1,0:T(8,128)(2,1)} broadcast(bf16[2,2,256,256]{3,2,1,0:T(8,128)(2,1)S(1)} %bitcast.254), dimensions={1,2,3,4} | broadcast | bytes 8912896 | tf_op jit(solution)/shard_map/stack | solution.py:67
  33.4 5.9 %all-to-all-start.1 = ((bf16[16,2,2,256,256]{4,3,2,1,0:T(8,128)(2,1)}), bf16[16,2,2,256,256]{4,3,2,1,0:T(8,128)(2,1)}, u32[]{:S(2)}, u32[]{:S(2)}) async-start(bf16[16,2,2,256,256]{4,3,2,1,0:T(8,128)(2,1)} %stack.18), calls=%async_computation.1 | async-start | bytes 16777216 | tf_op jit(solution)/shard_map/all_to_all | solution.py:67
  39.5 93.9 %all-to-all-done.1 = bf16[16,2,2,256,256]{4,3,2,1,0:T(8,128)(2,1)} async-done(((bf16[16,2,2,256,256]{4,3,2,1,0:T(8,128)(2,1)}), bf16[16,2,2,256,256]{4,3,2,1,0:T(8,128)(2,1)}, u32[]{:S(2)}, u32[]{:S(2)}) %all-to-all-start.1) | async-done | bytes 8388640 | tf_op jit(solution)/shard_map/all_to_all | solution.py:67
  133.5 5.1 %fusion.126 = (bf16[1,2,256,16,256]{4,2,1,0,3:T(8,128)(2,1)S(1)}, bf16[1,2,256,16,256]{4,2,1,0,3:T(8,128)(2,1)}) fusion(bf16[2,2,256,16,256]{4,2,1,0,3:T(8,128)(2,1)} %bitcast.3), kind=kLoop, calls=%fused_computation.129 | loop fusion | bytes 16777216 | tf_op jit(solution)/shard_map/slice | solution.py:70
  138.6 4.4 %copy.96 = bf16[1,2,256,16,256]{4,3,2,1,0:T(8,128)(2,1)} copy(bf16[1,2,256,16,256]{4,2,1,0,3:T(8,128)(2,1)S(1)} %get-tuple-element.25) | data formatting | bytes 8388608 | tf_op jit(solution)/shard_map/slice | solution.py:70
  143.0 7.4 %squeeze.16 = bf16[2,256,4096]{2,1,0:T(8,128)(2,1)} reshape(bf16[1,2,256,16,256]{4,3,2,1,0:T(8,128)(2,1)} %copy.96) | data formatting | bytes 8388608 | tf_op jit(solution)/shard_map/squeeze | solution.py:70
  150.4 3.6 %fusion.42 = bf16[2,256,256]{2,1,0:T(8,128)(2,1)S(1)} fusion(bf16[2,256,4096]{2,1,0:T(8,128)(2,1)} %squeeze.16, bf16[1,4096,256]{2,1,0:T(8,128)(2,1)S(1)} %copy-done), kind=kOutput, calls=%fused_computation.50 | convolution fusion | flops 1073872896 | bytes 6553600 | tf_op jit(solution)/shard_map/ekd,dc->ekc/dot_general | solution.py:71
  167.9 5.6 %all-to-all-start.2 = ((bf16[16,256,2,256]{3,1,2,0:T(8,128)(2,1)}), bf16[16,256,2,256]{3,1,2,0:T(8,128)(2,1)}, u32[]{:S(2)}, u32[]{:S(2)}) async-start(bf16[16,256,2,256]{3,1,2,0:T(8,128)(2,1)} %copy.115), calls=%async_computation.2 | async-start | bytes 8388608 | tf_op jit(solution)/shard_map/all_to_all | solution.py:104
  173.5 6.5 %copy.100 = bf16[1,2,256,16,256]{4,3,2,1,0:T(8,128)(2,1)} copy(bf16[1,2,256,16,256]{4,2,1,0,3:T(8,128)(2,1)} %get-tuple-element.26) | data formatting | bytes 8388608 | tf_op jit(solution)/shard_map/slice | solution.py:70
  180.0 7.4 %squeeze.19 = bf16[2,256,4096]{2,1,0:T(8,128)(2,1)} reshape(bf16[1,2,256,16,256]{4,3,2,1,0:T(8,128)(2,1)} %copy.100) | data formatting | bytes 8388608 | tf_op jit(solution)/shard_map/squeeze | solution.py:70
  187.4 4.2 %fusion.39 = bf16[2,256,256]{2,1,0:T(8,128)(2,1)S(1)} fusion(bf16[2,256,4096]{2,1,0:T(8,128)(2,1)} %squeeze.19, bf16[1,4096,256]{2,1,0:T(8,128)(2,1)} %param.13), kind=kOutput, calls=%fused_computation.49 | convolution fusion | flops 1073872896 | bytes 6553600 | tf_op jit(solution)/shard_map/ekd,dc->ekc/dot_general | solution.py:74
  205.3 17.4 %all-to-all-done.2 = bf16[16,256,2,256]{3,1,2,0:T(8,128)(2,1)} async-done(((bf16[16,256,2,256]{3,1,2,0:T(8,128)(2,1)}), bf16[16,256,2,256]{3,1,2,0:T(8,128)(2,1)}, u32[]{:S(2)}, u32[]{:S(2)}) %all-to-all-start.2) | async-done | bytes 4194336 | tf_op jit(solution)/shard_map/all_to_all | solution.py:104
  222.7 5.6 %all-to-all-start.3 = ((bf16[16,256,2,256]{3,1,2,0:T(8,128)(2,1)}), bf16[16,256,2,256]{3,1,2,0:T(8,128)(2,1)}, u32[]{:S(2)}, u32[]{:S(2)}) async-start(bf16[16,256,2,256]{3,1,2,0:T(8,128)(2,1)} %copy.118), calls=%async_computation.3 | async-start | bytes 8388608 | tf_op jit(solution)/shard_map/all_to_all | solution.py:104
  228.4 3.0 fusion.52
  231.4 2.8 fusion.53
  238.7 2.8 convert_reduce_fusion.1
  241.9 35.7 %all-to-all-done.3 = bf16[16,256,2,256]{3,1,2,0:T(8,128)(2,1)} async-done(((bf16[16,256,2,256]{3,1,2,0:T(8,128)(2,1)}), bf16[16,256,2,256]{3,1,2,0:T(8,128)(2,1)}, u32[]{:S(2)}, u32[]{:S(2)}) %all-to-all-start.3) | async-done | bytes 4194336 | tf_op jit(solution)/shard_map/all_to_all | solution.py:104
  277.6 2.8 convert_reduce_fusion
  282.4 4.7 %all-to-all-start.4 = ((f32[16,2,2,16,256]{4,2,3,1,0:T(2,128)}), f32[16,2,2,16,256]{4,2,3,1,0:T(2,128)S(1)}, u32[]{:S(2)}, u32[]{:S(2)}) async-start(f32[16,2,2,16,256]{4,2,3,1,0:T(2,128)} %maximum_bitcast_fusion), calls=%async_computation.4 | async-start | bytes 2097152 | tf_op jit(solution)/shard_map/all_to_all | solution.py:117
  295.0 3.7 %convolution_bitcast_fusion.2 = f32[256,4096]{1,0:T(8,128)S(1)} fusion(bf16[2,256,256]{2,1,0:T(8,128)(2,1)} %copy-done.10, bf16[2,256,4096]{2,1,0:T(8,128)(2,1)} %squeeze.19), kind=kOutput, calls=%fused_computation.10 | convolution fusion | flops 1073741824 | bytes 8650752 | tf_op jit(solution)/shard_map/ekd,ekc->dc/dot_general | solution.py:89
  301.3 4.1 %copy.124 = bf16[1,4096,256]{2,1,0:T(8,128)(2,1)} copy(bf16[1,4096,256]{1,2,0:T(8,128)(2,1)} %fusion.8) | data formatting | bytes 4194304
  305.4 3.6 %convolution_bitcast_fusion = f32[256,4096]{1,0:T(8,128)S(1)} fusion(bf16[2,256,4096]{2,1,0:T(8,128)(2,1)} %squeeze.19, bf16[2,256,256]{2,1,0:T(8,128)(2,1)S(1)} %convolution_convert_fusion), kind=kOutput, calls=%fused_computation.8 | convolution fusion | flops 1073741824 | bytes 8650752 | tf_op jit(solution)/shard_map/ekd,ekc->dc/dot_general | solution.py:92
  311.6 4.1 %copy.125 = bf16[1,4096,256]{2,1,0:T(8,128)(2,1)} copy(bf16[1,4096,256]{1,2,0:T(8,128)(2,1)} %fusion.9) | data formatting | bytes 4194304
  (80 shorter events, 51.8 us)
Async XLA Ops:
  0.6 149.8 %copy-start = (bf16[1,4096,256]{2,1,0:T(8,128)(2,1)S(1)}, bf16[1,4096,256]{2,1,0:T(8,128)(2,1)}, u32[]{:S(2)}) copy-start(bf16[1,4096,256]{2,1,0:T(8,128)(2,1)} %param.12) | copy-start | bytes 6291460
  33.4 5.9 %copy-start.16 = (s32[2,2]{1,0:T(2,128)S(1)}, s32[2,2]{1,0:T(2,128)}, u32[]{:S(2)}) copy-start(s32[2,2]{1,0:T(2,128)} %param.8) | copy-start | bytes 52
  33.4 5.9 %copy-start.17 = (s32[2,2]{1,0:T(2,128)S(1)}, s32[2,2]{1,0:T(2,128)}, u32[]{:S(2)}) copy-start(s32[2,2]{1,0:T(2,128)} %param.9) | copy-start | bytes 52
  33.4 100.0 %all-to-all-start.1 = ((bf16[16,2,2,256,256]{4,3,2,1,0:T(8,128)(2,1)}), bf16[16,2,2,256,256]{4,3,2,1,0:T(8,128)(2,1)}, u32[]{:S(2)}, u32[]{:S(2)}) async-start(bf16[16,2,2,256,256]{4,3,2,1,0:T(8,128)(2,1)} %stack.18), calls=%async_computation.1 | async-start | bytes 16777216 | tf_op jit(solution)/shard_map/all_to_all | solution.py:67
  150.4 3.6 %copy-start.2 = (bf16[2,256,4096]{2,1,0:T(8,128)(2,1)S(1)}, bf16[2,256,4096]{2,1,0:T(8,128)(2,1)}, u32[]{:S(2)}) copy-start(bf16[2,256,4096]{2,1,0:T(8,128)(2,1)} %squeeze.16) | copy-start | bytes 12582916
  150.4 4.1 %copy-start.5 = (bf16[1,4096,256]{2,1,0:T(8,128)(2,1)S(1)}, bf16[1,4096,256]{2,1,0:T(8,128)(2,1)}, u32[]{:S(2)}) copy-start(bf16[1,4096,256]{2,1,0:T(8,128)(2,1)} %param.13) | copy-start | bytes 6291460
  154.5 4.3 %copy-start.20 = (bf16[2,256,256]{2,1,0:T(8,128)(2,1)}, bf16[2,256,256]{2,1,0:T(8,128)(2,1)S(1)}, u32[]{:S(2)}) copy-start(bf16[2,256,256]{2,1,0:T(8,128)(2,1)S(1)} %fusion.42) | copy-start | bytes 786436
  154.5 2.0 copy-start.13
  154.5 3.1 copy-start.18
  160.4 3.6 %copy-start.8 = (bf16[2,256,256]{2,1,0:T(8,128)(2,1)}, bf16[2,256,256]{2,1,0:T(8,128)(2,1)S(1)}, u32[]{:S(2)}) copy-start(bf16[2,256,256]{2,1,0:T(8,128)(2,1)S(1)} %convolution_convert_fusion.1) | copy-start | bytes 786436
  162.7 1.7 copy-start.6
  167.9 54.8 %all-to-all-start.2 = ((bf16[16,256,2,256]{3,1,2,0:T(8,128)(2,1)}), bf16[16,256,2,256]{3,1,2,0:T(8,128)(2,1)}, u32[]{:S(2)}, u32[]{:S(2)}) async-start(bf16[16,256,2,256]{3,1,2,0:T(8,128)(2,1)} %copy.115), calls=%async_computation.2 | async-start | bytes 8388608 | tf_op jit(solution)/shard_map/all_to_all | solution.py:104
  187.4 5.4 %copy-start.1 = (bf16[2,256,4096]{2,1,0:T(8,128)(2,1)S(1)}, bf16[2,256,4096]{2,1,0:T(8,128)(2,1)}, u32[]{:S(2)}) copy-start(bf16[2,256,4096]{2,1,0:T(8,128)(2,1)} %squeeze.19) | copy-start | bytes 12582916
  194.1 2.2 copy-start.21
  198.4 3.1 copy-start.10
  200.1 1.6 copy-start.7
  222.7 54.8 %all-to-all-start.3 = ((bf16[16,256,2,256]{3,1,2,0:T(8,128)(2,1)}), bf16[16,256,2,256]{3,1,2,0:T(8,128)(2,1)}, u32[]{:S(2)}, u32[]{:S(2)}) async-start(bf16[16,256,2,256]{3,1,2,0:T(8,128)(2,1)} %copy.118), calls=%async_computation.3 | async-start | bytes 8388608 | tf_op jit(solution)/shard_map/all_to_all | solution.py:104
  228.3 5.8 %copy-start.15 = (bf16[2,256,256]{2,1,0:T(8,128)(2,1)S(1)}, bf16[2,256,256]{2,1,0:T(8,128)(2,1)}, u32[]{:S(2)}) copy-start(bf16[2,256,256]{2,1,0:T(8,128)(2,1)} %copy-done.14) | copy-start | bytes 786436
  228.4 5.8 %copy-start.19 = (bf16[1,2,2,256,256]{4,3,2,1,0:T(8,128)(2,1)S(1)}, bf16[1,2,2,256,256]{4,3,2,1,0:T(8,128)(2,1)}, u32[]{:S(2)}) copy-start(bf16[1,2,2,256,256]{4,3,2,1,0:T(8,128)(2,1)} %param.10) | copy-start | bytes 1572868
  282.4 35.4 %all-to-all-start.4 = ((f32[16,2,2,16,256]{4,2,3,1,0:T(2,128)}), f32[16,2,2,16,256]{4,2,3,1,0:T(2,128)S(1)}, u32[]{:S(2)}, u32[]{:S(2)}) async-start(f32[16,2,2,16,256]{4,2,3,1,0:T(2,128)} %maximum_bitcast_fusion), calls=%async_computation.4 | async-start | bytes 2097152 | tf_op jit(solution)/shard_map/all_to_all | solution.py:117
  295.0 3.7 %copy-start.3 = (bf16[2,256,4096]{2,1,0:T(8,128)(2,1)S(1)}, bf16[2,256,4096]{2,1,0:T(8,128)(2,1)}, u32[]{:S(2)}) copy-start(bf16[2,256,4096]{2,1,0:T(8,128)(2,1)} %squeeze.16) | copy-start | bytes 12582916
  295.0 3.7 %copy-start.12 = (bf16[2,256,256]{2,1,0:T(8,128)(2,1)S(1)}, bf16[2,256,256]{2,1,0:T(8,128)(2,1)}, u32[]{:S(2)}) copy-start(bf16[2,256,256]{2,1,0:T(8,128)(2,1)} %copy-done.11) | copy-start | bytes 786436
  305.4 3.6 %copy-start.4 = (bf16[2,256,4096]{2,1,0:T(8,128)(2,1)S(1)}, bf16[2,256,4096]{2,1,0:T(8,128)(2,1)}, u32[]{:S(2)}) copy-start(bf16[2,256,4096]{2,1,0:T(8,128)(2,1)} %squeeze.16) | copy-start | bytes 12582916
  305.4 3.6 %copy-start.9 = (bf16[2,256,256]{2,1,0:T(8,128)(2,1)S(1)}, bf16[2,256,256]{2,1,0:T(8,128)(2,1)}, u32[]{:S(2)}) copy-start(bf16[2,256,256]{2,1,0:T(8,128)(2,1)} %copy-done.8) | copy-start | bytes 786436
  (2 other events, 2.0 us)
